TPU v7x, 512 devices: a whole 4x4x16 slice. The times are simulated.
512 devices in a mesh: row: 32 (over z, y_lo), col: 16 (over x, y_hi, core).
Axes of the slice: x: 4, y: 4 (y_hi: 2, y_lo: 2; y = y_hi * 2 + y_lo), z: 16, core: 2. Of those that a mesh axis runs over, the one named last changes fastest.
Arguments:
- inputs: bfloat16 [1, 256, 256, 1024], P(None, 'row', 'col'), may hold values from -6 to 6
- norm_gain: float32 [1024], replicated, may hold values from 0.1 to 1.9
- w_query: bfloat16 [1024, 512], P('row'), may hold values from -8 to 8
- w_keyvalue: bfloat16 [1024, 1024], P('row'), may hold values from -0.1875 to 0.1875
- w_output: bfloat16 [512, 1024], P('row'), may hold values from -0.25 to 0.25
- out_grad: bfloat16 [1, 256, 256, 1024], P(None, 'row', 'col'), may hold values from -6 to 6
Outputs:
- layer_out: bfloat16 [1, 256, 256, 1024], P(None, 'row', 'col')
- in_grad: bfloat16 [1, 256, 256, 1024], P(None, 'row', 'col')
- keyvalue_grad: float32 [1024, 1024], P('row')
All inputs are finite; a program needn't handle non-finite values.
Results may differ from a plain program's by a relative error of at most 0.012.
The roundings to bfloat16 on the way count: a program that leaves them out, or rounds other values in their place, can miss the bound.
Values may be sent and summed in bfloat16 or wider, within the bound.
No kernel may reach another device: no remote copies, remote signals or barrier semaphores. Data moves between devices by JAX's collectives and lax.ppermute only.
A program may use at most 64 MiB of HBM per device.

v0:
```python
import math
import jax
import jax.numpy as jnp
from jax import lax
from jax.sharding import PartitionSpec as P

HEADS = 8
RADIUS = 6
EPS = 1e-05
MASKED = -1e30


def shifted(value, axis, steps):
    count = lax.axis_size(axis)
    first, last = (max(0, -steps), min(count, count - steps))
    return lax.ppermute(value, axis, [(source, source + steps) for source in range(first, last)])


def with_halo(block, sides, width):
    for axis, dim in sides:
        count = lax.axis_size(axis)
        forward = [(i, i + 1) for i in range(count - 1)]
        backward = [(target, source) for source, target in forward]
        low = lax.ppermute(
            lax.slice_in_dim(block, block.shape[dim] - width, None, axis=dim), axis, forward
        )
        high = lax.ppermute(lax.slice_in_dim(block, 0, width, axis=dim), axis, backward)
        block = jnp.concatenate([low, block, high], axis=dim)
    return block


def normalize(inputs, norm_gain):
    values = inputs.astype(jnp.float32)
    center = values - jnp.mean(values, axis=-1, keepdims=True)
    spread = lax.rsqrt(jnp.mean(center * center, axis=-1, keepdims=True) + EPS)
    standard = center * spread
    return (standard, spread, (standard * norm_gain).astype(jnp.bfloat16))


def window_mask(row_start, col_start, tile_rows, tile_cols, height, map_width):
    ext_rows = tile_rows + 2 * RADIUS
    ext_cols = tile_cols + 2 * RADIUS
    query_pos = jnp.arange(tile_rows * tile_cols, dtype=jnp.int32)
    query_row = query_pos // tile_cols
    query_col = query_pos % tile_cols
    ext_pos = jnp.arange(ext_rows * ext_cols, dtype=jnp.int32)
    ext_row = ext_pos // ext_cols
    ext_col = ext_pos % ext_cols
    nearby = (jnp.abs(ext_row[None, :] - RADIUS - query_row[:, None]) <= RADIUS) & (
        jnp.abs(ext_col[None, :] - RADIUS - query_col[:, None]) <= RADIUS
    )
    global_row = row_start + ext_row - RADIUS
    global_col = col_start + ext_col - RADIUS
    inside = (
        (global_row >= 0) & (global_row < height) & (global_col >= 0) & (global_col < map_width)
    )
    return nearby & inside[None, :]


def tile_forward(queries, keyvalue_ext, allowed):
    batches, query_count, inner_width = queries.shape
    head_size = inner_width // HEADS
    query_heads = queries.reshape(batches, query_count, HEADS, head_size)
    key_heads = keyvalue_ext[:, :, :inner_width].reshape(batches, -1, HEADS, head_size)
    value_heads = keyvalue_ext[:, :, inner_width:].reshape(batches, -1, HEADS, head_size)
    scores = jnp.einsum(
        "bqhd,bkhd->bhqk", query_heads, key_heads, preferred_element_type=jnp.float32
    ) / math.sqrt(head_size)
    scores = jnp.where(allowed, scores, MASKED)
    row_max = jnp.max(scores, axis=-1, keepdims=True)
    exponent = jnp.exp(scores - row_max)
    soft = exponent / jnp.sum(exponent, axis=-1, keepdims=True)
    rounded = soft.astype(jnp.bfloat16)
    attended = jnp.einsum(
        "bhqk,bkhd->bqhd", rounded, value_heads, preferred_element_type=jnp.float32
    )
    return (attended.astype(jnp.bfloat16).reshape(batches, query_count, inner_width), soft, rounded)


def tile_backward(queries, keyvalue_ext, soft, rounded, inner_grad):
    batches, query_count, inner_width = queries.shape
    head_size = inner_width // HEADS
    query_heads = queries.reshape(batches, query_count, HEADS, head_size)
    key_heads = keyvalue_ext[:, :, :inner_width].reshape(batches, -1, HEADS, head_size)
    value_heads = keyvalue_ext[:, :, inner_width:].reshape(batches, -1, HEADS, head_size)
    grad_heads = inner_grad.reshape(batches, query_count, HEADS, head_size)
    prob_grad = jnp.einsum(
        "bqhd,bkhd->bhqk", grad_heads, value_heads, preferred_element_type=jnp.float32
    )
    row_dot = jnp.sum(soft * prob_grad, axis=-1, keepdims=True)
    score_grad = (soft * (prob_grad - row_dot) / math.sqrt(head_size)).astype(jnp.bfloat16)
    query_grad = jnp.einsum(
        "bhqk,bkhd->bqhd", score_grad, key_heads, preferred_element_type=jnp.float32
    )
    key_grad = jnp.einsum(
        "bhqk,bqhd->bkhd", score_grad, query_heads, preferred_element_type=jnp.float32
    )
    value_grad = jnp.einsum(
        "bhqk,bqhd->bkhd", rounded, grad_heads, preferred_element_type=jnp.float32
    )
    ext_count = key_grad.shape[1]
    joined = jnp.concatenate(
        [
            key_grad.reshape(batches, ext_count, inner_width),
            value_grad.reshape(batches, ext_count, inner_width),
        ],
        axis=-1,
    )
    return (query_grad.astype(jnp.bfloat16).reshape(batches, query_count, inner_width), joined)


def fold_cols(extended):
    left_strip = extended[:, :, :RADIUS]
    right_strip = extended[:, :, extended.shape[2] - RADIUS :]
    middle = extended[:, :, RADIUS : extended.shape[2] - RADIUS]
    from_right = shifted(left_strip, "col", -1)
    from_left = shifted(right_strip, "col", 1)
    inner_cols = middle.shape[2]
    return (
        middle
        + jnp.pad(from_left, ((0, 0), (0, 0), (0, inner_cols - RADIUS), (0, 0)))
        + jnp.pad(from_right, ((0, 0), (0, 0), (inner_cols - RADIUS, 0), (0, 0)))
    )


def fold_rows(extended):
    upper_strip = extended[:, :RADIUS]
    lower_strip = extended[:, extended.shape[1] - RADIUS :]
    middle = extended[:, RADIUS : extended.shape[1] - RADIUS]
    from_below = shifted(upper_strip, "row", -1)
    from_above = shifted(lower_strip, "row", 1)
    inner_rows = middle.shape[1]
    return (
        middle
        + jnp.pad(from_above, ((0, 0), (0, inner_rows - RADIUS), (0, 0), (0, 0)))
        + jnp.pad(from_below, ((0, 0), (inner_rows - RADIUS, 0), (0, 0), (0, 0)))
    )


def local(inputs, norm_gain, w_query, w_keyvalue, w_output, out_grad):
    batches, tile_rows, tile_cols, model_width = inputs.shape
    ext_rows = tile_rows + 2 * RADIUS
    ext_cols = tile_cols + 2 * RADIUS
    standard, spread, normed = normalize(inputs, norm_gain)
    flat_norm = normed.reshape(-1, model_width)
    full_query, full_keyvalue, full_output = (
        lax.all_gather(w_query, "row", axis=0, tiled=True),
        lax.all_gather(w_keyvalue, "row", axis=0, tiled=True),
        lax.all_gather(w_output, "row", axis=0, tiled=True),
    )
    inner_width = full_query.shape[1]
    queries = jnp.dot(flat_norm, full_query, preferred_element_type=jnp.float32).astype(
        jnp.bfloat16
    )
    queries = queries.reshape(batches, tile_rows * tile_cols, inner_width)
    keyvalue = jnp.dot(flat_norm, full_keyvalue, preferred_element_type=jnp.float32).astype(
        jnp.bfloat16
    )
    keyvalue = keyvalue.reshape(batches, tile_rows, tile_cols, 2 * inner_width)
    keyvalue_ext = with_halo(keyvalue, (("row", 1), ("col", 2)), RADIUS)
    keyvalue_ext = keyvalue_ext.reshape(batches, ext_rows * ext_cols, 2 * inner_width)
    allowed = window_mask(
        lax.axis_index("row") * tile_rows,
        lax.axis_index("col") * tile_cols,
        tile_rows,
        tile_cols,
        tile_rows * lax.axis_size("row"),
        tile_cols * lax.axis_size("col"),
    )
    attended, soft, rounded = tile_forward(queries, keyvalue_ext, allowed)
    projected = jnp.dot(
        attended.reshape(-1, inner_width), full_output, preferred_element_type=jnp.float32
    )
    layer_out = (inputs.astype(jnp.float32) + projected.reshape(inputs.shape)).astype(jnp.bfloat16)
    flat_grad = out_grad.reshape(-1, model_width)
    inner_grad = lax.dot_general(
        flat_grad, full_output, (((1,), (1,)), ((), ())), preferred_element_type=jnp.float32
    ).astype(jnp.bfloat16)
    inner_grad = inner_grad.reshape(batches, tile_rows * tile_cols, inner_width)
    query_grad, keyvalue_part = tile_backward(queries, keyvalue_ext, soft, rounded, inner_grad)
    keyvalue_part = keyvalue_part.reshape(batches, ext_rows, ext_cols, 2 * inner_width)
    owned = fold_rows(fold_cols(keyvalue_part))
    token_grad = owned.astype(jnp.bfloat16).reshape(-1, 2 * inner_width)
    rows_part = lax.psum_scatter(
        lax.dot_general(
            flat_norm, token_grad, (((0,), (0,)), ((), ())), preferred_element_type=jnp.float32
        ),
        "row",
        scatter_dimension=0,
        tiled=True,
    )
    keyvalue_grad = lax.psum(rows_part, "col")
    normed_grad = lax.dot_general(
        query_grad.reshape(-1, inner_width),
        full_query,
        (((1,), (1,)), ((), ())),
        preferred_element_type=jnp.float32,
    )
    normed_grad = normed_grad + lax.dot_general(
        token_grad, full_keyvalue, (((1,), (1,)), ((), ())), preferred_element_type=jnp.float32
    )
    gained = normed_grad.reshape(inputs.shape) * norm_gain
    in_grad = out_grad.astype(jnp.float32) + spread * (
        gained
        - jnp.mean(gained, axis=-1, keepdims=True)
        - standard * jnp.mean(gained * standard, axis=-1, keepdims=True)
    )
    return (layer_out, in_grad.astype(jnp.bfloat16), keyvalue_grad)


def solution(mesh):
    return jax.shard_map(
        local,
        mesh=mesh,
        in_specs=(
            P(None, "row", "col", None),
            P(),
            P("row", None),
            P("row", None),
            P("row", None),
            P(None, "row", "col", None),
        ),
        out_specs=(P(None, "row", "col", None), P(None, "row", "col", None), P("row", None)),
        check_vma=False,
    )
```

profile of v0, /device:TPU:1, one launch (start us, length us, event | category | flops | bytes accessed | tf_op | source)
XLA Modules:
  0.0 792.2 jit_solution(14434119171756185005)
XLA Ops:
  7.2 0.7 all-gather.4.cloned.1.call-update
  7.9 0.7 all-gather.8.cloned.1.call-update
  8.7 0.7 all-gather.6.cloned.1.call-update
  9.5 1.1 convert_reduce_fusion
  10.6 1.1 fusion.41
  11.8 0.3 fusion.45
  12.1 1.2 fusion.35
  13.3 115.3 %all-gather.4.cloned.1.call-done = bf16[1024,1024]{1,0:T(8,128)(2,1)} async-done(((bf16[32,1024]{1,0:T(8,128)(2,1)}), bf16[1024,1024]{1,0:T(8,128)(2,1)}) %all-gather.4.cloned.1.call-update) | async-done | bytes 2097168 | tf_op jit(solution)/shard_map/all_gather | solution.py:148
  128.6 2.0 convolution_convert_fusion
  130.7 2.2 collective-permute-start
  132.9 1.3 collective-permute-start.1
  134.2 126.6 %all-gather.8.cloned.1.call-done = bf16[512,1024]{1,0:T(8,128)(2,1)} async-done(((bf16[16,1024]{1,0:T(8,128)(2,1)}), bf16[512,1024]{1,0:T(8,128)(2,1)}) %all-gather.8.cloned.1.call-update) | async-done | bytes 1048592 | tf_op jit(solution)/shard_map/all_gather | solution.py:149
  260.8 1.7 convolution_convert_fusion.1
  262.5 0.1 copy.29
  262.7 0.1 pad_maximum_fusion.1
  262.7 0.1 fusion.73
  262.9 26.0 %collective-permute-start.2 = (bf16[1,20,6,1024]{3,2,1,0:T(8,128)(2,1)S(1)}, bf16[1,20,6,1024]{3,2,1,0:T(8,128)(2,1)S(1)}, u32[]{:S(2)}, u32[]{:S(2)}) collective-permute-start(bf16[1,20,6,1024]{3,2,1,0:T(8,128)(2,1)S(1)} %get-tuple-element.9), channel_id=1, source_target_pairs={{0,1},{1,2},{2,3},{3,4},{4,5},{5,6},{6,7},{7,8},{8,9},{9,10},{10,1... | collective-permute-start | bytes 737288 | tf_op jit(solution)/shard_map/ppermute | solution.py:24
  288.8 1.9 collective-permute-start.3
  290.8 102.0 %all-gather.6.cloned.1.call-done = bf16[1024,512]{1,0:T(8,128)(2,1)} async-done(((bf16[32,512]{1,0:T(8,128)(2,1)}), bf16[1024,512]{1,0:T(8,128)(2,1)}) %all-gather.6.cloned.1.call-update) | async-done | bytes 1048592 | tf_op jit(solution)/shard_map/all_gather | solution.py:147
  392.8 1.5 convolution_convert_fusion.2
  394.3 0.1 copy.26
  394.5 0.6 pad_maximum_fusion
  395.1 0.3 reshape.242
  395.4 0.1 fusion.72
  395.5 0.3 copy.35
  395.8 0.3 copy.34
  396.1 2.0 fusion.76
  398.1 2.3 fusion.75
  400.5 2.3 convolution_bitcast_fusion.1
  402.8 2.5 copy.31
  405.4 1.4 concatenate.17
  406.8 5.7 fusion.12
  412.4 2.5 copy.30
  415.0 2.4 concatenate.16
  417.4 2.5 constant_dynamic-update-slice_fusion.1
  419.9 1.0 constant_dynamic-update-slice_fusion
  420.9 0.7 fusion.70
  421.6 26.0 %collective-permute-start.4 = (f32[1,20,6,1024]{3,0,2,1:T(1,128)S(1)}, f32[1,20,6,1024]{3,0,2,1:T(1,128)S(1)}, u32[]{:S(2)}, u32[]{:S(2)}) collective-permute-start(f32[1,20,6,1024]{3,0,2,1:T(1,128)S(1)} %get-tuple-element.3), channel_id=1, source_target_pairs={{0,1},{1,2},{2,3},{3,4},{4,5},{5,6},{6,7},{7,8},{8,9},{9,10},{10,1... | collective-permute-start | bytes 1474568 | tf_op jit(solution)/shard_map/ppermute | solution.py:16
  447.5 2.1 collective-permute-start.5
  449.7 9.1 %collective-permute-done.4 = f32[1,20,6,1024]{3,0,2,1:T(1,128)S(1)} collective-permute-done((f32[1,20,6,1024]{3,0,2,1:T(1,128)S(1)}, f32[1,20,6,1024]{3,0,2,1:T(1,128)S(1)}, u32[]{:S(2)}, u32[]{:S(2)}) %collective-permute-start.4) | collective-permute-done | bytes 491552 | tf_op jit(solution)/shard_map/ppermute | solution.py:16
  458.7 0.5 collective-permute-done.5
  459.2 1.5 fusion.15
  460.7 0.5 fusion.71
  461.2 1.3 collective-permute-start.6
  462.5 1.3 collective-permute-start.7
  463.8 11.6 %collective-permute-done.6 = f32[1,6,16,1024]{3,0,2,1:T(1,128)S(1)} collective-permute-done((f32[1,6,16,1024]{3,0,2,1:T(1,128)S(1)}, f32[1,6,16,1024]{3,0,2,1:T(1,128)S(1)}, u32[]{:S(2)}, u32[]{:S(2)}) %collective-permute-start.6) | collective-permute-done | bytes 393248 | tf_op jit(solution)/shard_map/ppermute | solution.py:16
  475.4 0.6 fusion.43
  476.1 0.1 copy.32
  476.2 0.7 copy-done.10
  476.9 2.7 convolution_bitcast_fusion
  479.6 1.0 copy-done.5
  480.6 2.3 fusion.26
  483.0 0.2 copy.28
  483.2 0.2 reshape.246
  483.4 5.5 fusion.18
  489.0 1.0 fusion.17
  490.0 1.8 fusion.77
  491.8 0.6 multiply_reduce_fusion.1
  492.4 0.1 div.62
  492.5 0.3 fusion.36
  492.7 116.1 %reduce-scatter.2.cloned.1.call-done = f32[32,1024]{1,0:T(8,128)} async-done(((f32[1024,1024]{1,0:T(8,128)}), f32[32,1024]{1,0:T(8,128)}) %reduce-scatter.2.cloned.1.call-update) | async-done | bytes 131088 | tf_op jit(solution)/shard_map/reduce_scatter | solution.py:184
  608.8 1.0 fusion.40
  609.8 174.3 %all-reduce.6.cloned.1.call-done = f32[32,1024]{1,0:T(8,128)} async-done(((f32[32,1024]{1,0:T(8,128)}), f32[32,1024]{1,0:T(8,128)}) %all-reduce.6.cloned.1.call-update) | async-done | bytes 131088 | tf_op jit(solution)/shard_map/psum | solution.py:192
  784.1 1.6 copy.38
  (50 shorter events, 0.4 us)
Async XLA Ops:
  7.2 121.5 %all-gather.4.cloned.1.call-start = ((), (), s32[]{:S(2)}) async-start(), calls=%async_computation.1 | async-start | bytes 2162688 | tf_op jit(solution)/shard_map/all_gather | solution.py:148
  7.9 252.9 %all-gather.8.cloned.1.call-start = ((), (), s32[]{:S(2)}) async-start(), calls=%async_computation.3 | async-start | bytes 1081344 | tf_op jit(solution)/shard_map/all_gather | solution.py:149
  8.6 384.1 %all-gather.6.cloned.1.call-start = ((), (), s32[]{:S(2)}) async-start(), calls=%async_computation.2 | async-start | bytes 1081344 | tf_op jit(solution)/shard_map/all_gather | solution.py:147
  9.4 599.4 %reduce-scatter.2.cloned.1.call-start = ((), (), s32[]{:S(2)}) async-start(), calls=%async_computation.4 | async-start | bytes 4325376 | tf_op jit(solution)/shard_map/reduce_scatter | solution.py:184
  9.5 251.3 %copy-start.8 = (bf16[1,8,16,1024]{3,2,1,0:T(8,128)(2,1)S(1)}, bf16[1,8,16,1024]{3,2,1,0:T(8,128)(2,1)}, u32[]{:S(2)}) copy-start(bf16[1,8,16,1024]{3,2,1,0:T(8,128)(2,1)} %param.11) | copy-start | bytes 786436
  13.3 379.5 %copy-start.6 = (bf16[1,8,16,1024]{3,2,1,0:T(8,128)(2,1)}, bf16[1,8,16,1024]{3,2,1,0:T(8,128)(2,1)S(1)}, u32[]{:S(2)}) copy-start(bf16[1,8,16,1024]{3,2,1,0:T(8,128)(2,1)S(1)} %fusion.35) | copy-start | bytes 786436
  130.7 131.9 %collective-permute-start = (bf16[1,6,16,1024]{3,2,1,0:T(8,128)(2,1)S(1)}, bf16[1,6,16,1024]{3,2,1,0:T(8,128)(2,1)S(1)}, u32[]{:S(2)}, u32[]{:S(2)}) collective-permute-start(bf16[1,6,16,1024]{3,2,1,0:T(8,128)(2,1)S(1)} %get-tuple-element.11), channel_id=1, source_target_pairs={{0,16},{16,32},{32,48},{48,64},{64,80},{80,96},{96,112},{112,128},... | collective-permute-start | bytes 589832 | tf_op jit(solution)/shard_map/ppermute | solution.py:24
  132.9 129.8 %collective-permute-start.1 = (bf16[1,6,16,1024]{3,2,1,0:T(8,128)(2,1)S(1)}, bf16[1,6,16,1024]{3,2,1,0:T(8,128)(2,1)S(1)}, u32[]{:S(2)}, u32[]{:S(2)}) collective-permute-start(bf16[1,6,16,1024]{3,2,1,0:T(8,128)(2,1)S(1)} %get-tuple-element.12), channel_id=1, source_target_pairs={{16,0},{32,16},{48,32},{64,48},{80,64},{96,80},{112,96},{128,112},... | collective-permute-start | bytes 589832 | tf_op jit(solution)/shard_map/ppermute | solution.py:27
  262.9 131.6 %collective-permute-start.2 = (bf16[1,20,6,1024]{3,2,1,0:T(8,128)(2,1)S(1)}, bf16[1,20,6,1024]{3,2,1,0:T(8,128)(2,1)S(1)}, u32[]{:S(2)}, u32[]{:S(2)}) collective-permute-start(bf16[1,20,6,1024]{3,2,1,0:T(8,128)(2,1)S(1)} %get-tuple-element.9), channel_id=1, source_target_pairs={{0,1},{1,2},{2,3},{3,4},{4,5},{5,6},{6,7},{7,8},{8,9},{9,10},{10,1... | collective-permute-start | bytes 737288 | tf_op jit(solution)/shard_map/ppermute | solution.py:24
  288.8 105.7 %collective-permute-start.3 = (bf16[1,20,6,1024]{3,2,1,0:T(8,128)(2,1)S(1)}, bf16[1,20,6,1024]{3,2,1,0:T(8,128)(2,1)S(1)}, u32[]{:S(2)}, u32[]{:S(2)}) collective-permute-start(bf16[1,20,6,1024]{3,2,1,0:T(8,128)(2,1)S(1)} %get-tuple-element.10), channel_id=1, source_target_pairs={{1,0},{2,1},{3,2},{4,3},{5,4},{6,5},{7,6},{8,7},{9,8},{10,9},{11,1... | collective-permute-start | bytes 737288 | tf_op jit(solution)/shard_map/ppermute | solution.py:27
  394.5 6.0 copy-start.13
  395.8 4.7 copy-start.11
  396.1 4.4 copy-start.4
  421.6 37.2 %collective-permute-start.4 = (f32[1,20,6,1024]{3,0,2,1:T(1,128)S(1)}, f32[1,20,6,1024]{3,0,2,1:T(1,128)S(1)}, u32[]{:S(2)}, u32[]{:S(2)}) collective-permute-start(f32[1,20,6,1024]{3,0,2,1:T(1,128)S(1)} %get-tuple-element.3), channel_id=1, source_target_pairs={{0,1},{1,2},{2,3},{3,4},{4,5},{5,6},{6,7},{7,8},{8,9},{9,10},{10,1... | collective-permute-start | bytes 1474568 | tf_op jit(solution)/shard_map/ppermute | solution.py:16
  447.5 11.7 %collective-permute-start.5 = (f32[1,20,6,1024]{3,0,2,1:T(1,128)S(1)}, f32[1,20,6,1024]{3,0,2,1:T(1,128)S(1)}, u32[]{:S(2)}, u32[]{:S(2)}) collective-permute-start(f32[1,20,6,1024]{3,0,2,1:T(1,128)S(1)} %get-tuple-element.4), channel_id=1, source_target_pairs={{1,0},{2,1},{3,2},{4,3},{5,4},{6,5},{7,6},{8,7},{9,8},{10,9},{11,1... | collective-permute-start | bytes 1474568 | tf_op jit(solution)/shard_map/ppermute | solution.py:16
  460.7 16.2 %copy-start.7 = (bf16[1,8,16,1024]{3,2,1,0:T(8,128)(2,1)S(1)}, bf16[1,8,16,1024]{3,2,1,0:T(8,128)(2,1)}, u32[]{:S(2)}) copy-start(bf16[1,8,16,1024]{3,2,1,0:T(8,128)(2,1)} %copy-done.6) | copy-start | bytes 786436
  461.2 14.2 %collective-permute-start.6 = (f32[1,6,16,1024]{3,0,2,1:T(1,128)S(1)}, f32[1,6,16,1024]{3,0,2,1:T(1,128)S(1)}, u32[]{:S(2)}, u32[]{:S(2)}) collective-permute-start(f32[1,6,16,1024]{3,0,2,1:T(1,128)S(1)} %get-tuple-element.5), channel_id=1, source_target_pairs={{0,16},{16,32},{32,48},{48,64},{64,80},{80,96},{96,112},{112,128},... | collective-permute-start | bytes 1179656 | tf_op jit(solution)/shard_map/ppermute | solution.py:16
  462.5 12.9 %collective-permute-start.7 = (f32[1,6,16,1024]{3,0,2,1:T(1,128)S(1)}, f32[1,6,16,1024]{3,0,2,1:T(1,128)S(1)}, u32[]{:S(2)}, u32[]{:S(2)}) collective-permute-start(f32[1,6,16,1024]{3,0,2,1:T(1,128)S(1)} %get-tuple-element.6), channel_id=1, source_target_pairs={{16,0},{32,16},{48,32},{64,48},{80,64},{96,80},{112,96},{128,112},... | collective-permute-start | bytes 1179656 | tf_op jit(solution)/shard_map/ppermute | solution.py:16
  476.2 0.7 copy-start.10
  479.5 1.1 copy-start.5
  479.5 1.1 copy-start.14
  479.6 304.6 %all-reduce.6.cloned.1.call-start = ((), (), s32[]{:S(2)}) async-start(), calls=%async_computation.5 | async-start | bytes 262144 | tf_op jit(solution)/shard_map/psum | solution.py:192
  483.4 5.6 copy-start
  483.4 5.6 copy-start.3
  483.4 6.6 copy-start.1
  488.9 2.8 copy-start.2
  489.0 2.9 copy-start.12
  489.0 2.8 copy-start.15
  491.8 117.1 %copy-start.9 = (bf16[1,8,16,1024]{3,2,1,0:T(8,128)(2,1)S(1)}, bf16[1,8,16,1024]{3,2,1,0:T(8,128)(2,1)}, u32[]{:S(2)}) copy-start(bf16[1,8,16,1024]{3,2,1,0:T(8,128)(2,1)} %param.11) | copy-start | bytes 786436
Sparse Core Ops, SparseCore 0:
  10.1 118.4 all-gather.3
  130.7 130.0 all-gather.7
  262.9 129.8 all-gather.5
  479.7 129.0 reduce-scatter.1
  611.5 172.5 all-reduce.5
where the time goes:
time: 793 us; the launch traced here: 792 us
  waiting for transfers between devices  658 us (83%)
  starting transfers between devices  62.2 us (8%)
  matrix products  31.5 us (4%)
  local copies, waits for them, and re-layouts  18.8 us (2%)
  between operations  14.3 us (2%)
    psum x1, waiting for transfers between devices, local(): keyvalue_grad = lax.psum(rows_part, 'col')  174 us
    all_gather x1, waiting for transfers between devices, local(): lax.all_gather(w_output, 'row', axis=0, tiled=True)  127 us
    reduce_scatter x1, waiting for transfers between devices, local(): lax.psum_scatter(lax.dot_general(flat_norm, token_grad, (((0,), (0,)), ((...  116 us
    all_gather x1, waiting for transfers between devices, local(): lax.all_gather(w_keyvalue, 'row', axis=0, tiled=True)  115 us
    all_gather x1, waiting for transfers between devices, local(): lax.all_gather(w_query, 'row', axis=0, tiled=True)  102 us
    ppermute x4, starting transfers between devices, shifted(): lax.ppermute(value, axis, [(source, source + steps) for source in range(f...  30.7 us
    ppermute x2, starting transfers between devices, with_halo(): lax.ppermute(lax.slice_in_dim(block, block.shape[dim] - width, None, axis...  28.1 us
    ppermute x4, waiting for transfers between devices, shifted(): lax.ppermute(value, axis, [(source, source + steps) for source in range(f...  21.1 us
  transfers between devices with their start and end apart: 13, of which 8 were waited for; matrix products, arithmetic and copies ran while one was open for 3% of the time, Pallas kernels for 0%

commit v1 on v0

--- a/solution.py
+++ b/solution.py
@@ -8,6 +8,10 @@
 RADIUS = 6
 EPS = 1e-05
 MASKED = -1e30
+
+
+def guide_roads(array_in):
+    return jnp.sum(lax.all_gather(array_in, "col"), axis=0)
 
 
 def shifted(value, axis, steps):
@@ -189,7 +193,7 @@
         scatter_dimension=0,
         tiled=True,
     )
-    keyvalue_grad = lax.psum(rows_part, "col")
+    keyvalue_grad = guide_roads(rows_part)
     normed_grad = lax.dot_general(
         query_grad.reshape(-1, inner_width),
         full_query,

time: 793 us -> 706 us (0.89)
  waiting for transfers between devices: 658 us -> 571 us
    psum x1 -> x0, waiting for transfers between devices: 174 us -> none  [local(): keyvalue_grad = lax.psum(rows_part, 'col')]
    all_gather x0 -> x1, waiting for transfers between devices: none -> 75 us  [guide_roads(): return jnp.sum(lax.all_gather(array_in, 'col'), axis=0)]
    reduce_scatter x1, waiting for transfers between devices: 116 us -> 129 us  [local(): lax.psum_scatter(lax.dot_general(flat_norm, token_grad, (((0,), (0,)), ((...]
where the time goes in v1:
time: 706 us
  waiting for transfers between devices  571 us (81%)
  starting transfers between devices  62.2 us (9%)
  matrix products  31.5 us (4%)
  local copies, waits for them, and re-layouts  16.2 us (2%)
  between operations  14.3 us (2%)
  other arithmetic  10.2 us (1%)
    reduce_scatter x1, waiting for transfers between devices, local(): lax.psum_scatter(lax.dot_general(flat_norm, token_grad, (((0,), (0,)), ((...  129 us
    all_gather x1, waiting for transfers between devices, local(): lax.all_gather(w_output, 'row', axis=0, tiled=True)  127 us
    all_gather x1, waiting for transfers between devices, local(): lax.all_gather(w_keyvalue, 'row', axis=0, tiled=True)  115 us
    all_gather x1, waiting for transfers between devices, local(): lax.all_gather(w_query, 'row', axis=0, tiled=True)  102 us
    all_gather x1, waiting for transfers between devices, guide_roads(): return jnp.sum(lax.all_gather(array_in, 'col'), axis=0)  75 us
    ppermute x4, starting transfers between devices, shifted(): lax.ppermute(value, axis, [(source, source + steps) for source in range(f...  30.7 us
    ppermute x2, starting transfers between devices, with_halo(): lax.ppermute(lax.slice_in_dim(block, block.shape[dim] - width, None, axis...  28.1 us
    ppermute x4, waiting for transfers between devices, shifted(): lax.ppermute(value, axis, [(source, source + steps) for source in range(f...  21.1 us
  transfers between devices with their start and end apart: 13, of which 8 were waited for; matrix products, arithmetic and copies ran while one was open for 3% of the time, Pallas kernels for 0%

profile of v1, /device:TPU:1, one launch (start us, length us, event | category | flops | bytes accessed | tf_op | source)
XLA Modules:
  0.0 705.8 jit_solution(13289561855208643378)
XLA Ops:
  7.2 0.7 all-gather.6.cloned.1.call-update
  7.9 0.7 all-gather.10.cloned.1.call-update
  8.7 0.7 all-gather.8.cloned.1.call-update
  9.5 1.1 convert_reduce_fusion
  10.6 1.1 fusion.41
  11.8 0.3 fusion.45
  12.1 1.2 fusion.35
  13.3 115.3 %all-gather.6.cloned.1.call-done = bf16[1024,1024]{1,0:T(8,128)(2,1)} async-done(((bf16[32,1024]{1,0:T(8,128)(2,1)}), bf16[1024,1024]{1,0:T(8,128)(2,1)}) %all-gather.6.cloned.1.call-update) | async-done | bytes 2097168 | tf_op jit(solution)/shard_map/all_gather | solution.py:152
  128.6 2.0 convolution_convert_fusion
  130.7 2.2 collective-permute-start
  132.9 1.3 collective-permute-start.1
  134.2 126.6 %all-gather.10.cloned.1.call-done = bf16[512,1024]{1,0:T(8,128)(2,1)} async-done(((bf16[16,1024]{1,0:T(8,128)(2,1)}), bf16[512,1024]{1,0:T(8,128)(2,1)}) %all-gather.10.cloned.1.call-update) | async-done | bytes 1048592 | tf_op jit(solution)/shard_map/all_gather | solution.py:153
  260.8 1.7 convolution_convert_fusion.1
  262.5 0.1 copy.29
  262.7 0.1 pad_maximum_fusion.1
  262.7 0.1 fusion.73
  262.9 26.0 %collective-permute-start.2 = (bf16[1,20,6,1024]{3,2,1,0:T(8,128)(2,1)S(1)}, bf16[1,20,6,1024]{3,2,1,0:T(8,128)(2,1)S(1)}, u32[]{:S(2)}, u32[]{:S(2)}) collective-permute-start(bf16[1,20,6,1024]{3,2,1,0:T(8,128)(2,1)S(1)} %get-tuple-element.9), channel_id=1, source_target_pairs={{0,1},{1,2},{2,3},{3,4},{4,5},{5,6},{6,7},{7,8},{8,9},{9,10},{10,1... | collective-permute-start | bytes 737288 | tf_op jit(solution)/shard_map/ppermute | solution.py:28
  288.8 1.9 collective-permute-start.3
  290.8 102.0 %all-gather.8.cloned.1.call-done = bf16[1024,512]{1,0:T(8,128)(2,1)} async-done(((bf16[32,512]{1,0:T(8,128)(2,1)}), bf16[1024,512]{1,0:T(8,128)(2,1)}) %all-gather.8.cloned.1.call-update) | async-done | bytes 1048592 | tf_op jit(solution)/shard_map/all_gather | solution.py:151
  392.8 1.5 convolution_convert_fusion.2
  394.3 0.1 copy.26
  394.5 0.6 pad_maximum_fusion
  395.1 0.3 reshape.242
  395.4 0.1 fusion.72
  395.5 0.3 copy.35
  395.8 0.3 copy.34
  396.1 2.0 fusion.76
  398.1 2.3 fusion.75
  400.5 2.3 convolution_bitcast_fusion.1
  402.8 2.5 copy.31
  405.4 1.4 concatenate.17
  406.8 5.7 fusion.12
  412.4 2.5 copy.30
  415.0 2.4 concatenate.16
  417.4 2.5 constant_dynamic-update-slice_fusion.1
  419.9 1.0 constant_dynamic-update-slice_fusion
  420.9 0.7 fusion.70
  421.6 26.0 %collective-permute-start.4 = (f32[1,20,6,1024]{3,0,2,1:T(1,128)S(1)}, f32[1,20,6,1024]{3,0,2,1:T(1,128)S(1)}, u32[]{:S(2)}, u32[]{:S(2)}) collective-permute-start(f32[1,20,6,1024]{3,0,2,1:T(1,128)S(1)} %get-tuple-element.3), channel_id=1, source_target_pairs={{0,1},{1,2},{2,3},{3,4},{4,5},{5,6},{6,7},{7,8},{8,9},{9,10},{10,1... | collective-permute-start | bytes 1474568 | tf_op jit(solution)/shard_map/ppermute | solution.py:20
  447.5 2.1 collective-permute-start.5
  449.7 9.1 %collective-permute-done.4 = f32[1,20,6,1024]{3,0,2,1:T(1,128)S(1)} collective-permute-done((f32[1,20,6,1024]{3,0,2,1:T(1,128)S(1)}, f32[1,20,6,1024]{3,0,2,1:T(1,128)S(1)}, u32[]{:S(2)}, u32[]{:S(2)}) %collective-permute-start.4) | collective-permute-done | bytes 491552 | tf_op jit(solution)/shard_map/ppermute | solution.py:20
  458.7 0.5 collective-permute-done.5
  459.2 1.5 fusion.15
  460.7 0.5 fusion.71
  461.2 1.3 collective-permute-start.6
  462.5 1.3 collective-permute-start.7
  463.8 11.6 %collective-permute-done.6 = f32[1,6,16,1024]{3,0,2,1:T(1,128)S(1)} collective-permute-done((f32[1,6,16,1024]{3,0,2,1:T(1,128)S(1)}, f32[1,6,16,1024]{3,0,2,1:T(1,128)S(1)}, u32[]{:S(2)}, u32[]{:S(2)}) %collective-permute-start.6) | collective-permute-done | bytes 393248 | tf_op jit(solution)/shard_map/ppermute | solution.py:20
  475.4 0.6 fusion.43
  476.1 0.1 copy.32
  476.2 0.7 copy-done.10
  476.9 2.7 convolution_bitcast_fusion
  479.6 0.0 all-gather.12.cloned.1.call-start
  479.6 129.2 %reduce-scatter.2.cloned.1.call-done = f32[32,1024]{1,0:T(8,128)} async-done(((f32[1024,1024]{1,0:T(8,128)}), f32[32,1024]{1,0:T(8,128)}) %reduce-scatter.2.cloned.1.call-update) | async-done | bytes 131088 | tf_op jit(solution)/shard_map/reduce_scatter | solution.py:188
  608.8 2.3 fusion.26
  611.2 0.2 copy.28
  611.4 0.2 reshape.246
  611.6 5.5 fusion.18
  617.2 1.0 fusion.17
  618.2 1.8 fusion.77
  620.1 0.6 multiply_reduce_fusion.1
  620.6 0.1 div.62
  620.7 0.3 fusion.36
  621.0 1.0 fusion.40
  622.0 75.0 %all-gather.12.cloned.1.call-done = f32[512,1024]{1,0:T(8,128)} async-done(((f32[32,1024]{1,0:T(8,128)}), f32[512,1024]{1,0:T(8,128)}) %all-gather.12.cloned.1.call-update) | async-done | bytes 2097168 | tf_op jit(solution)/shard_map/all_gather | solution.py:14
  696.9 2.4 reduce_sum.69
  (50 shorter events, 0.4 us)
Async XLA Ops:
  7.2 121.5 %all-gather.6.cloned.1.call-start = ((), (), s32[]{:S(2)}) async-start(), calls=%async_computation.1 | async-start | bytes 2162688 | tf_op jit(solution)/shard_map/all_gather | solution.py:152
  7.9 252.9 %all-gather.10.cloned.1.call-start = ((), (), s32[]{:S(2)}) async-start(), calls=%async_computation.3 | async-start | bytes 1081344 | tf_op jit(solution)/shard_map/all_gather | solution.py:153
  8.6 384.1 %all-gather.8.cloned.1.call-start = ((), (), s32[]{:S(2)}) async-start(), calls=%async_computation.2 | async-start | bytes 1081344 | tf_op jit(solution)/shard_map/all_gather | solution.py:151
  9.4 599.4 %reduce-scatter.2.cloned.1.call-start = ((), (), s32[]{:S(2)}) async-start(), calls=%async_computation.4 | async-start | bytes 4325376 | tf_op jit(solution)/shard_map/reduce_scatter | solution.py:188
  9.5 251.3 %copy-start.8 = (bf16[1,8,16,1024]{3,2,1,0:T(8,128)(2,1)S(1)}, bf16[1,8,16,1024]{3,2,1,0:T(8,128)(2,1)}, u32[]{:S(2)}) copy-start(bf16[1,8,16,1024]{3,2,1,0:T(8,128)(2,1)} %param.11) | copy-start | bytes 786436
  13.3 379.5 %copy-start.6 = (bf16[1,8,16,1024]{3,2,1,0:T(8,128)(2,1)}, bf16[1,8,16,1024]{3,2,1,0:T(8,128)(2,1)S(1)}, u32[]{:S(2)}) copy-start(bf16[1,8,16,1024]{3,2,1,0:T(8,128)(2,1)S(1)} %fusion.35) | copy-start | bytes 786436
  130.7 131.9 %collective-permute-start = (bf16[1,6,16,1024]{3,2,1,0:T(8,128)(2,1)S(1)}, bf16[1,6,16,1024]{3,2,1,0:T(8,128)(2,1)S(1)}, u32[]{:S(2)}, u32[]{:S(2)}) collective-permute-start(bf16[1,6,16,1024]{3,2,1,0:T(8,128)(2,1)S(1)} %get-tuple-element.11), channel_id=1, source_target_pairs={{0,16},{16,32},{32,48},{48,64},{64,80},{80,96},{96,112},{112,128},... | collective-permute-start | bytes 589832 | tf_op jit(solution)/shard_map/ppermute | solution.py:28
  132.9 129.8 %collective-permute-start.1 = (bf16[1,6,16,1024]{3,2,1,0:T(8,128)(2,1)S(1)}, bf16[1,6,16,1024]{3,2,1,0:T(8,128)(2,1)S(1)}, u32[]{:S(2)}, u32[]{:S(2)}) collective-permute-start(bf16[1,6,16,1024]{3,2,1,0:T(8,128)(2,1)S(1)} %get-tuple-element.12), channel_id=1, source_target_pairs={{16,0},{32,16},{48,32},{64,48},{80,64},{96,80},{112,96},{128,112},... | collective-permute-start | bytes 589832 | tf_op jit(solution)/shard_map/ppermute | solution.py:31
  262.9 131.6 %collective-permute-start.2 = (bf16[1,20,6,1024]{3,2,1,0:T(8,128)(2,1)S(1)}, bf16[1,20,6,1024]{3,2,1,0:T(8,128)(2,1)S(1)}, u32[]{:S(2)}, u32[]{:S(2)}) collective-permute-start(bf16[1,20,6,1024]{3,2,1,0:T(8,128)(2,1)S(1)} %get-tuple-element.9), channel_id=1, source_target_pairs={{0,1},{1,2},{2,3},{3,4},{4,5},{5,6},{6,7},{7,8},{8,9},{9,10},{10,1... | collective-permute-start | bytes 737288 | tf_op jit(solution)/shard_map/ppermute | solution.py:28
  288.8 105.7 %collective-permute-start.3 = (bf16[1,20,6,1024]{3,2,1,0:T(8,128)(2,1)S(1)}, bf16[1,20,6,1024]{3,2,1,0:T(8,128)(2,1)S(1)}, u32[]{:S(2)}, u32[]{:S(2)}) collective-permute-start(bf16[1,20,6,1024]{3,2,1,0:T(8,128)(2,1)S(1)} %get-tuple-element.10), channel_id=1, source_target_pairs={{1,0},{2,1},{3,2},{4,3},{5,4},{6,5},{7,6},{8,7},{9,8},{10,9},{11,1... | collective-permute-start | bytes 737288 | tf_op jit(solution)/shard_map/ppermute | solution.py:31
  394.5 6.0 copy-start.13
  395.8 4.7 copy-start.11
  396.1 4.4 copy-start.4
  421.6 37.2 %collective-permute-start.4 = (f32[1,20,6,1024]{3,0,2,1:T(1,128)S(1)}, f32[1,20,6,1024]{3,0,2,1:T(1,128)S(1)}, u32[]{:S(2)}, u32[]{:S(2)}) collective-permute-start(f32[1,20,6,1024]{3,0,2,1:T(1,128)S(1)} %get-tuple-element.3), channel_id=1, source_target_pairs={{0,1},{1,2},{2,3},{3,4},{4,5},{5,6},{6,7},{7,8},{8,9},{9,10},{10,1... | collective-permute-start | bytes 1474568 | tf_op jit(solution)/shard_map/ppermute | solution.py:20
  447.5 11.7 %collective-permute-start.5 = (f32[1,20,6,1024]{3,0,2,1:T(1,128)S(1)}, f32[1,20,6,1024]{3,0,2,1:T(1,128)S(1)}, u32[]{:S(2)}, u32[]{:S(2)}) collective-permute-start(f32[1,20,6,1024]{3,0,2,1:T(1,128)S(1)} %get-tuple-element.4), channel_id=1, source_target_pairs={{1,0},{2,1},{3,2},{4,3},{5,4},{6,5},{7,6},{8,7},{9,8},{10,9},{11,1... | collective-permute-start | bytes 1474568 | tf_op jit(solution)/shard_map/ppermute | solution.py:20
  460.7 16.2 %copy-start.7 = (bf16[1,8,16,1024]{3,2,1,0:T(8,128)(2,1)S(1)}, bf16[1,8,16,1024]{3,2,1,0:T(8,128)(2,1)}, u32[]{:S(2)}) copy-start(bf16[1,8,16,1024]{3,2,1,0:T(8,128)(2,1)} %copy-done.6) | copy-start | bytes 786436
  461.2 14.2 %collective-permute-start.6 = (f32[1,6,16,1024]{3,0,2,1:T(1,128)S(1)}, f32[1,6,16,1024]{3,0,2,1:T(1,128)S(1)}, u32[]{:S(2)}, u32[]{:S(2)}) collective-permute-start(f32[1,6,16,1024]{3,0,2,1:T(1,128)S(1)} %get-tuple-element.5), channel_id=1, source_target_pairs={{0,16},{16,32},{32,48},{48,64},{64,80},{80,96},{96,112},{112,128},... | collective-permute-start | bytes 1179656 | tf_op jit(solution)/shard_map/ppermute | solution.py:20
  462.5 12.9 %collective-permute-start.7 = (f32[1,6,16,1024]{3,0,2,1:T(1,128)S(1)}, f32[1,6,16,1024]{3,0,2,1:T(1,128)S(1)}, u32[]{:S(2)}, u32[]{:S(2)}) collective-permute-start(f32[1,6,16,1024]{3,0,2,1:T(1,128)S(1)} %get-tuple-element.6), channel_id=1, source_target_pairs={{16,0},{32,16},{48,32},{64,48},{80,64},{96,80},{112,96},{128,112},... | collective-permute-start | bytes 1179656 | tf_op jit(solution)/shard_map/ppermute | solution.py:20
  476.2 0.7 copy-start.10
  479.5 129.3 %copy-start.5 = (bf16[1,560,512]{1,2,0:T(8,128)(2,1)S(1)}, bf16[1,560,512]{1,2,0:T(8,128)(2,1)}, u32[]{:S(2)}) copy-start(bf16[1,560,512]{1,2,0:T(8,128)(2,1)} %copy-done.4) | copy-start | bytes 1720324
  479.5 129.3 %copy-start.14 = (bf16[128,512]{0,1:T(8,128)(2,1)S(1)}, bf16[128,512]{0,1:T(8,128)(2,1)}, u32[]{:S(2)}) copy-start(bf16[128,512]{0,1:T(8,128)(2,1)} %copy-done.13) | copy-start | bytes 393220
  479.6 217.4 %all-gather.12.cloned.1.call-start = ((), (), s32[]{:S(2)}) async-start(), calls=%async_computation.5 | async-start | bytes 2228224 | tf_op jit(solution)/shard_map/all_gather | solution.py:14
  611.6 5.6 copy-start
  611.6 5.6 copy-start.3
  611.6 6.6 copy-start.1
  617.2 2.9 copy-start.2
  617.2 2.9 copy-start.12
  617.2 2.9 copy-start.15
  618.2 2.8 copy-start.9
Sparse Core Ops, SparseCore 0:
  10.1 118.4 all-gather.5
  130.7 130.0 all-gather.9
  262.9 129.8 all-gather.7
  479.7 129.0 reduce-scatter.1
  611.9 84.9 all-gather.11
